TPU v7x, 32 devices: a whole 2x2x4 slice. The times are simulated.
32 devices in a mesh: mem: 8 (over y, x, core), tile: 4 (over z).
Axes of the slice: x: 2, y: 2, z: 4, core: 2. Of those that a mesh axis runs over, the one named last changes fastest.
Arguments:
- perturb: bfloat16 [40, 2, 2, 256, 512], P('mem', None, None, None, 'tile'), may hold values from -6 to 6
- coef_x: float32 [2, 256, 512], P(None, None, 'tile'), may hold values from 0.25 to 0.5
- coef_y: float32 [2, 256, 512], P(None, None, 'tile'), may hold values from 0.25 to 0.5
- obs_values: float32 [65536], P(('mem', 'tile')), may hold values from -12 to 12
- obs_tile: int32 [65536, 1], P(('mem', 'tile')), may hold values from 0 to 3; in each aligned block of 2048 rows (0 to 2047, 2048 to 4095, ...) at most 1536 rows name the same one
- obs_cell: int32 [65536], P(('mem', 'tile')), may hold values from 0 to 131071
Outputs:
- increment: float32 [256, 2, 2, 512], P('mem', None, None, 'tile')
Inputs may be any that keep to these rules, and one draw needn't show every extreme that they name: `obs_tile`: among the 2048 observations of one device no tile is named more than 1536 times, and in every draw some device names some tile exactly 1536 times.
All inputs are finite; a program needn't handle non-finite values.
Results may differ from a plain program's by a relative error of at most 0.0003.
Values sent between devices are 32-bit elements; how exact they have to be, the bound alone decides.
No kernel may reach another device: no remote copies, remote signals or barrier semaphores. Data moves between devices by JAX's collectives and lax.ppermute only.
A program may use at most 64 MiB of HBM per device.

v0:
```python
import jax
import jax.numpy as jnp
from jax import lax
from jax.sharding import PartitionSpec as P

FIELDS = 2
LEVELS = 2
SWEEPS = 6
LAT = 256


def extended_2(block, sides, width):
    for axis, dim in sides:
        count = lax.axis_size(axis)
        forward = [(i, i + 1) for i in range(count - 1)]
        forward.append((count - 1, 0))
        backward = [(target, source) for source, target in forward]
        low = lax.ppermute(
            lax.slice_in_dim(block, block.shape[dim] - width, None, axis=dim), axis, forward
        )
        high = lax.ppermute(lax.slice_in_dim(block, 0, width, axis=dim), axis, backward)
        block = jnp.concatenate([low, block, high], axis=dim)
    return block


def sweep_east(field, coef):
    flux = coef[..., :-1] * (field[..., 1:] - field[..., :-1])
    return field[..., 1:-1] + flux[..., 1:] - flux[..., :-1]


def sweep_north(field, coef):
    flux = coef[..., :-1, :] * (field[..., 1:, :] - field[..., :-1, :])
    zero_row = jnp.zeros(field.shape[:-2] + (1, field.shape[-1]), jnp.float32)
    upper = jnp.concatenate([flux, zero_row], axis=-2)
    lower = jnp.concatenate([zero_row, flux], axis=-2)
    return field + upper - lower


def deposit(lists, total_cells):
    cells = lists[1].astype(jnp.int32)
    return jnp.zeros((total_cells,), jnp.float32).at[cells].add(lists[0])


def on_device(perturb, coef_x, coef_y, obs_values, obs_tile, obs_cell):
    tiles = lax.axis_size("tile")
    members = perturb.shape[0] * lax.axis_size("mem")
    lon_local = perturb.shape[4]
    capacity = 3 * obs_values.shape[0] // tiles
    total_cells = FIELDS * LEVELS * LAT * lon_local
    target = obs_tile[:, 0]
    onehot = (jnp.arange(tiles, dtype=jnp.int32)[:, None] == target[None, :]).astype(jnp.int32)
    before = jnp.cumsum(onehot, axis=1) - onehot
    ranking = jnp.sum(before * onehot, axis=0)
    slot = target * capacity + ranking
    packed = jnp.stack([obs_values, obs_cell.astype(jnp.float32)])
    outgoing = jnp.zeros((2, tiles * capacity), jnp.float32).at[:, slot].set(packed)
    incoming = lax.all_to_all(outgoing, "tile", split_axis=1, concat_axis=1, tiled=True)
    adjoint_field = lax.psum(deposit(incoming, total_cells), "mem")
    adjoint_field = adjoint_field.reshape(FIELDS, LEVELS, LAT, lon_local)
    widened = perturb.astype(jnp.float32)
    product = jnp.sum(widened * adjoint_field[None], axis=1)
    joined = jnp.concatenate([product, coef_x[None]], axis=0)
    padded = extended_2(joined, (("tile", 3),), 1)
    coef_wide = padded[-1]
    product = sweep_east(padded[:-1], coef_wide)
    for step in range(SWEEPS - 1):
        extended = extended_2(product, (("tile", 3),), 1)
        product = sweep_east(extended, coef_wide)
    for step in range(SWEEPS):
        product = sweep_north(product, coef_y)
    summed = lax.psum_scatter(
        jnp.einsum("kflyx,klyx->yflx", widened, product), "mem", scatter_dimension=0, tiled=True
    )
    return summed / (members - 1)


def solution(mesh):
    return jax.shard_map(
        on_device,
        mesh=mesh,
        in_specs=(
            P("mem", None, None, None, "tile"),
            P(None, None, "tile"),
            P(None, None, "tile"),
            P(("mem", "tile")),
            P(("mem", "tile"), None),
            P(("mem", "tile")),
        ),
        out_specs=P("mem", None, None, "tile"),
        check_vma=False,
    )
```

profile of v0, /device:TPU:0, one launch (start us, length us, event | category | flops | bytes accessed | tf_op | source)
XLA Modules:
  0.0 282.0 jit_solution(17903227486573302017)
XLA Ops:
  13.1 6.7 %scatter_custom_fusion = f32[2,6144]{0,1:T(8,128)S(1)} fusion(s32[2048]{0:T(1024)S(1)} %bitcast.51, f32[2048,2]{1,0:T(8,128)} %copy.13, f32[]{:T(128)} %constant.6.clone.1), kind=kCustom, calls=%fused_computation.22 | custom fusion | bytes 49664 | tf_op jit(solution)/shard_map/scatter | solution.py:56
  21.0 11.8 %all_to_all.9 = f32[2,4,1536]{2,0,1:T(2,128)S(1)} all-to-all(f32[2,4,1536]{2,0,1:T(2,128)S(1)} %copy.14), channel_id=1, replica_groups=mesh['mem'=8,'tile'=4] {'tile'}, dimensions={1} | all-to-all | bytes 98304 | tf_op jit(solution)/shard_map/all_to_all | solution.py:57
  32.9 41.0 %scatter_custom_fusion.1 = f32[131072]{0:T(1024)} fusion(s32[6144]{0:T(1024)S(1)} %bitcast.49, f32[6144]{0:T(1024)S(1)} %bitcast.50, f32[]{:T(128)} %constant.6.clone.1), kind=kCustom, calls=%fused_computation.59 | custom fusion | flops 6144 | bytes 524292 | tf_op jit(solution)/shard_map/scatter-add | solution.py:41
  74.0 54.7 %all-reduce.16.cloned.1.call-done = f32[2,2,256,128]{3,2,1,0:T(8,128)} async-done(((f32[2,2,256,128]{3,2,1,0:T(8,128)}), f32[2,2,256,128]{3,2,1,0:T(8,128)}) %all-reduce.16.cloned.1.call-update) | async-done | bytes 524304 | tf_op jit(solution)/shard_map/psum | solution.py:58
  128.6 1.9 multiply_reduce_fusion.1
  130.5 2.2 pad_maximum_fusion.4
  132.7 1.9 copy.15
  136.0 1.9 copy.16
  137.9 2.4 collective-permute-start.1
  140.3 1.7 copy.17
  142.0 1.7 copy.18
  148.4 1.7 copy.21
  150.1 3.8 %collective-permute-start.2 = (f32[5,2,256,1]{2,1,3,0:T(2,128)S(1)}, f32[5,2,256,1]{2,1,3,0:T(2,128)S(1)}, u32[]{:S(2)}, u32[]{:S(2)}) collective-permute-start(f32[5,2,256,1]{2,1,3,0:T(2,128)S(1)} %copy.21), channel_id=1, source_target_pairs={{1,0},{2,1},{3,2},{0,3},{5,4},{6,5},{7,6},{4,7},{9,8},{10,9},{11,1... | collective-permute-start | bytes 30728 | tf_op jit(solution)/shard_map/ppermute | solution.py:21
  155.7 4.1 %collective-permute-done.3 = f32[5,2,256,1]{2,1,3,0:T(2,128)S(1)} collective-permute-done((f32[5,2,256,1]{2,1,3,0:T(2,128)S(1)}, f32[5,2,256,1]{2,1,3,0:T(2,128)S(1)}, u32[]{:S(2)}, u32[]{:S(2)}) %collective-permute-start.3) | collective-permute-done | bytes 10272 | tf_op jit(solution)/shard_map/ppermute | solution.py:18
  161.3 2.1 fusion.2
  165.3 1.7 copy.25
  167.5 2.2 collective-permute-start.5
  171.1 2.0 collective-permute-done.5
  174.6 2.1 fusion.3
  178.6 1.7 copy.29
  180.8 2.0 collective-permute-start.7
  184.5 1.8 collective-permute-done.7
  187.8 2.1 fusion.4
  191.7 1.7 copy.33
  193.9 2.0 collective-permute-start.9
  197.6 1.8 collective-permute-done.9
  200.9 2.1 fusion.5
  204.9 1.7 copy.37
  207.0 2.2 collective-permute-start.11
  210.7 2.0 collective-permute-done.11
  214.3 2.1 fusion.6
  223.4 50.3 %all-reduce.18.cloned.1.call-done = f32[256,2,2,128]{3,2,1,0:T(2,128)} async-done(((f32[256,2,2,128]{3,2,1,0:T(2,128)}), f32[256,2,2,128]{3,2,1,0:T(2,128)}) %all-reduce.18.cloned.1.call-update) | async-done | bytes 524304
  (85 shorter events, 46.8 us)
Async XLA Ops:
  6.5 122.1 %all-reduce.16.cloned.1.call-start = ((), (), s32[]{:S(2)}) async-start(), calls=%async_computation.1 | async-start | bytes 1048576 | tf_op jit(solution)/shard_map/psum | solution.py:58
  73.9 56.6 %copy-start.4 = (f32[2,256,128]{2,1,0:T(8,128)S(1)}, f32[2,256,128]{2,1,0:T(8,128)}, u32[]{:S(2)}) copy-start(f32[2,256,128]{2,1,0:T(8,128)} %param.7) | copy-start | bytes 786436
  73.9 199.8 %all-reduce.18.cloned.1.call-start = ((), (), s32[]{:S(2)}) async-start(), calls=%async_computation.2 | async-start | bytes 1048576
  134.6 5.7 %collective-permute-start = (f32[6,2,256,1]{2,1,3,0:T(2,128)S(1)}, f32[6,2,256,1]{2,1,3,0:T(2,128)S(1)}, u32[]{:S(2)}, u32[]{:S(2)}) collective-permute-start(f32[6,2,256,1]{2,1,3,0:T(2,128)S(1)} %copy.15), channel_id=1, source_target_pairs={{0,1},{1,2},{2,3},{3,0},{4,5},{5,6},{6,7},{7,4},{8,9},{9,10},{10,1... | collective-permute-start | bytes 36872 | tf_op jit(solution)/shard_map/ppermute | solution.py:18
  137.9 4.1 %collective-permute-start.1 = (f32[6,2,256,1]{2,1,3,0:T(2,128)S(1)}, f32[6,2,256,1]{2,1,3,0:T(2,128)S(1)}, u32[]{:S(2)}, u32[]{:S(2)}) collective-permute-start(f32[6,2,256,1]{2,1,3,0:T(2,128)S(1)} %copy.16), channel_id=1, source_target_pairs={{1,0},{2,1},{3,2},{0,3},{5,4},{6,5},{7,6},{4,7},{9,8},{10,9},{11,1... | collective-permute-start | bytes 36872 | tf_op jit(solution)/shard_map/ppermute | solution.py:21
  143.7 1.6 copy-start
  143.7 2.0 copy-start.1
  150.1 5.2 %collective-permute-start.2 = (f32[5,2,256,1]{2,1,3,0:T(2,128)S(1)}, f32[5,2,256,1]{2,1,3,0:T(2,128)S(1)}, u32[]{:S(2)}, u32[]{:S(2)}) collective-permute-start(f32[5,2,256,1]{2,1,3,0:T(2,128)S(1)} %copy.21), channel_id=1, source_target_pairs={{1,0},{2,1},{3,2},{0,3},{5,4},{6,5},{7,6},{4,7},{9,8},{10,9},{11,1... | collective-permute-start | bytes 30728 | tf_op jit(solution)/shard_map/ppermute | solution.py:21
  154.3 5.5 %collective-permute-start.3 = (f32[5,2,256,1]{2,1,3,0:T(2,128)S(1)}, f32[5,2,256,1]{2,1,3,0:T(2,128)S(1)}, u32[]{:S(2)}, u32[]{:S(2)}) collective-permute-start(f32[5,2,256,1]{2,1,3,0:T(2,128)S(1)} %copy.23), channel_id=1, source_target_pairs={{0,1},{1,2},{2,3},{3,0},{4,5},{5,6},{6,7},{7,4},{8,9},{9,10},{10,1... | collective-permute-start | bytes 30728 | tf_op jit(solution)/shard_map/ppermute | solution.py:18
  167.0 3.7 %collective-permute-start.4 = (f32[5,2,256,1]{2,1,3,0:T(2,128)S(1)}, f32[5,2,256,1]{2,1,3,0:T(2,128)S(1)}, u32[]{:S(2)}, u32[]{:S(2)}) collective-permute-start(f32[5,2,256,1]{2,1,3,0:T(2,128)S(1)} %copy.25), channel_id=1, source_target_pairs={{1,0},{2,1},{3,2},{0,3},{5,4},{6,5},{7,6},{4,7},{9,8},{10,9},{11,1... | collective-permute-start | bytes 30728 | tf_op jit(solution)/shard_map/ppermute | solution.py:21
  167.5 5.7 %collective-permute-start.5 = (f32[5,2,256,1]{2,1,3,0:T(2,128)S(1)}, f32[5,2,256,1]{2,1,3,0:T(2,128)S(1)}, u32[]{:S(2)}, u32[]{:S(2)}) collective-permute-start(f32[5,2,256,1]{2,1,3,0:T(2,128)S(1)} %copy.27), channel_id=1, source_target_pairs={{0,1},{1,2},{2,3},{3,0},{4,5},{5,6},{6,7},{7,4},{8,9},{9,10},{10,1... | collective-permute-start | bytes 30728 | tf_op jit(solution)/shard_map/ppermute | solution.py:18
  180.3 3.7 %collective-permute-start.6 = (f32[5,2,256,1]{2,1,3,0:T(2,128)S(1)}, f32[5,2,256,1]{2,1,3,0:T(2,128)S(1)}, u32[]{:S(2)}, u32[]{:S(2)}) collective-permute-start(f32[5,2,256,1]{2,1,3,0:T(2,128)S(1)} %copy.29), channel_id=1, source_target_pairs={{1,0},{2,1},{3,2},{0,3},{5,4},{6,5},{7,6},{4,7},{9,8},{10,9},{11,1... | collective-permute-start | bytes 30728 | tf_op jit(solution)/shard_map/ppermute | solution.py:21
  180.8 5.5 %collective-permute-start.7 = (f32[5,2,256,1]{2,1,3,0:T(2,128)S(1)}, f32[5,2,256,1]{2,1,3,0:T(2,128)S(1)}, u32[]{:S(2)}, u32[]{:S(2)}) collective-permute-start(f32[5,2,256,1]{2,1,3,0:T(2,128)S(1)} %copy.31), channel_id=1, source_target_pairs={{0,1},{1,2},{2,3},{3,0},{4,5},{5,6},{6,7},{7,4},{8,9},{9,10},{10,1... | collective-permute-start | bytes 30728 | tf_op jit(solution)/shard_map/ppermute | solution.py:18
  193.4 3.7 %collective-permute-start.8 = (f32[5,2,256,1]{2,1,3,0:T(2,128)S(1)}, f32[5,2,256,1]{2,1,3,0:T(2,128)S(1)}, u32[]{:S(2)}, u32[]{:S(2)}) collective-permute-start(f32[5,2,256,1]{2,1,3,0:T(2,128)S(1)} %copy.33), channel_id=1, source_target_pairs={{1,0},{2,1},{3,2},{0,3},{5,4},{6,5},{7,6},{4,7},{9,8},{10,9},{11,1... | collective-permute-start | bytes 30728 | tf_op jit(solution)/shard_map/ppermute | solution.py:21
  193.9 5.5 %collective-permute-start.9 = (f32[5,2,256,1]{2,1,3,0:T(2,128)S(1)}, f32[5,2,256,1]{2,1,3,0:T(2,128)S(1)}, u32[]{:S(2)}, u32[]{:S(2)}) collective-permute-start(f32[5,2,256,1]{2,1,3,0:T(2,128)S(1)} %copy.35), channel_id=1, source_target_pairs={{0,1},{1,2},{2,3},{3,0},{4,5},{5,6},{6,7},{7,4},{8,9},{9,10},{10,1... | collective-permute-start | bytes 30728 | tf_op jit(solution)/shard_map/ppermute | solution.py:18
  206.6 3.7 %collective-permute-start.10 = (f32[5,2,256,1]{2,1,3,0:T(2,128)S(1)}, f32[5,2,256,1]{2,1,3,0:T(2,128)S(1)}, u32[]{:S(2)}, u32[]{:S(2)}) collective-permute-start(f32[5,2,256,1]{2,1,3,0:T(2,128)S(1)} %copy.37), channel_id=1, source_target_pairs={{1,0},{2,1},{3,2},{0,3},{5,4},{6,5},{7,6},{4,7},{9,8},{10,9},{11,1... | collective-permute-start | bytes 30728 | tf_op jit(solution)/shard_map/ppermute | solution.py:21
  207.0 5.7 %collective-permute-start.11 = (f32[5,2,256,1]{2,1,3,0:T(2,128)S(1)}, f32[5,2,256,1]{2,1,3,0:T(2,128)S(1)}, u32[]{:S(2)}, u32[]{:S(2)}) collective-permute-start(f32[5,2,256,1]{2,1,3,0:T(2,128)S(1)} %copy.39), channel_id=1, source_target_pairs={{0,1},{1,2},{2,3},{3,0},{4,5},{5,6},{6,7},{7,4},{8,9},{9,10},{10,1... | collective-permute-start | bytes 30728 | tf_op jit(solution)/shard_map/ppermute | solution.py:18
  216.3 1.0 copy-start.2
  219.3 1.3 copy-start.3
  220.9 1.2 copy-start.5
Sparse Core Ops, SparseCore 0:
  74.0 54.5 all-reduce.15
  222.3 51.3 all-reduce.17
where the time goes:
time: 283 us; the launch traced here: 282 us
  waiting for transfers between devices  122 us (43%)
  other arithmetic  68.9 us (24%)
  local copies, waits for them, and re-layouts  48.3 us (17%)
  starting transfers between devices  16.4 us (6%)
  between operations  14.4 us (5%)
  blocking collectives  11.8 us (4%)
    psum x1, waiting for transfers between devices, on_device(): adjoint_field = lax.psum(deposit(incoming, total_cells), 'mem')  54.7 us
    unnamed x3, waiting for transfers between devices  50.3 us
    scatter-add x1, other arithmetic, deposit(): return jnp.zeros((total_cells,), jnp.float32).at[cells].add(lists[0])  41 us
    all_to_all x1, blocking collectives, on_device(): lax.all_to_all(outgoing, 'tile', split_axis=1, concat_axis=1, tiled=True)  11.8 us
    ppermute x6, waiting for transfers between devices, extended_2(): lax.ppermute(lax.slice_in_dim(block, block.shape[dim] - width, None, axis...  11.7 us
    slice x11, local copies, waits for them, and re-layouts, extended_2(): lax.slice_in_dim(block, block.shape[dim] - width, None, axis=dim)  11.3 us
    mul x6, other arithmetic, sweep_east(): flux = coef[..., :-1] * (field[..., 1:] - field[..., :-1])  11 us
    slice x6, local copies, waits for them, and re-layouts, extended_2(): lax.slice_in_dim(block, 0, width, axis=dim)  10.4 us
  transfers between devices with their start and end apart: 14, of which 12 were waited for; matrix products, arithmetic and copies ran while one was open for 3% of the time, Pallas kernels for 0%

commit v1 on v0

v1 whole, which is shorter than its diff:
```python
import jax
import jax.numpy as jnp
from jax import lax
from jax.sharding import PartitionSpec as P

FIELDS = 2
LEVELS = 2
SWEEPS = 6
LAT = 256


def sweep_north(field, coef):
    flux = coef[..., :-1, :] * (field[..., 1:, :] - field[..., :-1, :])
    zero_row = jnp.zeros(field.shape[:-2] + (1, field.shape[-1]), jnp.float32)
    upper = jnp.concatenate([flux, zero_row], axis=-2)
    lower = jnp.concatenate([zero_row, flux], axis=-2)
    return field + upper - lower


def deposit(values, cells, rows, cols, width):
    index = cells.astype(jnp.int32)
    span = rows * cols
    channel = index // span
    remain = index % span
    row = remain // cols
    column = channel * cols + remain % cols
    row_hit = (row[:, None] == jnp.arange(rows, dtype=jnp.int32)[None, :]).astype(jnp.bfloat16)
    hit = column[:, None] == jnp.arange(width, dtype=jnp.int32)[None, :]
    rounded = lax.reduce_precision(values, exponent_bits=8, mantissa_bits=7)
    high = rounded.astype(jnp.bfloat16)
    low = (values - rounded).astype(jnp.bfloat16)
    zero = jnp.zeros((), jnp.bfloat16)
    weighted = jnp.concatenate(
        [jnp.where(hit, high[:, None], zero), jnp.where(hit, low[:, None], zero)], axis=1
    )
    both = jnp.einsum("nr,nj->rj", row_hit, weighted, preferred_element_type=jnp.float32)
    return both[:, :width] + both[:, width:]


def allreduce_mem(x, mems):
    bits = mems.bit_length() - 1
    assert 1 << bits == mems
    me = lax.axis_index("mem")
    for b in range(bits):
        pairs = [(i, i ^ (1 << b)) for i in range(mems)]
        mine = (me >> b) & 1
        halves = x.reshape((2, x.shape[0] // 2) + x.shape[1:])
        keep = lax.dynamic_index_in_dim(halves, mine, 0, keepdims=False)
        send = lax.dynamic_index_in_dim(halves, 1 - mine, 0, keepdims=False)
        x = keep + lax.ppermute(send, "mem", pairs)
    for b in reversed(range(bits)):
        pairs = [(i, i ^ (1 << b)) for i in range(mems)]
        mine = (me >> b) & 1
        other = lax.ppermute(x, "mem", pairs)
        out = jnp.zeros((2,) + x.shape, x.dtype)
        out = lax.dynamic_update_index_in_dim(out, x, mine, 0)
        out = lax.dynamic_update_index_in_dim(out, other, 1 - mine, 0)
        x = out.reshape((-1,) + x.shape[1:])
    return x


def on_device(perturb, coef_x, coef_y, obs_values, obs_tile, obs_cell):
    tiles = lax.axis_size("tile")
    mems = lax.axis_size("mem")
    kl, nf, nl, nr, nq = perturb.shape
    members = kl * mems
    width = nf * nl * nq
    halo = SWEEPS

    forward = [(i, (i + 1) % tiles) for i in range(tiles)]
    backward = [((i + 1) % tiles, i) for i in range(tiles)]
    coef_left = lax.ppermute(coef_x[..., -halo:], "tile", forward)
    coef_right = lax.ppermute(coef_x[..., :halo], "tile", backward)

    target = obs_tile[:, 0]
    dest = jnp.arange(tiles, dtype=jnp.int32)[:, None]
    values = jnp.where(target[None, :] == dest, obs_values[None, :], 0.0)
    cells = jnp.broadcast_to(obs_cell.astype(jnp.float32)[None, :], values.shape)
    outgoing = jnp.stack([values, cells], axis=1)
    incoming = lax.all_to_all(outgoing, "tile", 0, 0, tiled=True)
    field = deposit(incoming[0, 0], incoming[0, 1], nr, nq, width)
    for source in range(1, tiles):
        field = field + deposit(incoming[source, 0], incoming[source, 1], nr, nq, width)
    field = allreduce_mem(field, mems)
    adjoint = jnp.transpose(field.reshape(nr, nf, nl, nq), (1, 2, 0, 3))

    widened = perturb.astype(jnp.float32)
    product = jnp.sum(widened * adjoint[None], axis=1)
    left = lax.ppermute(product[..., -halo:], "tile", forward)
    right = lax.ppermute(product[..., :halo], "tile", backward)
    value = jnp.concatenate([left, product, right], axis=-1)
    coef = jnp.concatenate([coef_left, coef_x, coef_right], axis=-1)
    for step in range(SWEEPS):
        flux = coef[..., :-1] * (value[..., 1:] - value[..., :-1])
        value = value[..., 1:-1] + flux[..., 1:] - flux[..., :-1]
        coef = coef[..., 1:-1]
    product = value
    for step in range(SWEEPS):
        product = sweep_north(product, coef_y)
    part = jnp.einsum("kflyx,klyx->yflx", widened, product)
    blocks = part.reshape((mems, nr // mems) + part.shape[1:])
    summed = lax.all_to_all(blocks, "mem", 0, 0, tiled=True).sum(axis=0)
    return summed / (members - 1)


def solution(mesh):
    return jax.shard_map(
        on_device,
        mesh=mesh,
        in_specs=(
            P("mem", None, None, None, "tile"),
            P(None, None, "tile"),
            P(None, None, "tile"),
            P(("mem", "tile")),
            P(("mem", "tile"), None),
            P(("mem", "tile")),
        ),
        out_specs=P("mem", None, None, "tile"),
        check_vma=False,
    )
```

time: 283 us -> 113 us (0.40)
  waiting for transfers between devices: 122 us -> 27.4 us
  other arithmetic: 68.9 us -> 28.5 us
  local copies, waits for them, and re-layouts: 48.3 us -> 15.3 us
  between operations: 14.4 us -> 0.58 us
  matrix products: 0 us -> 6.63 us
  starting transfers between devices: 16.4 us -> 20.4 us
    psum x1 -> x0, waiting for transfers between devices: 54.7 us -> none  [on_device(): adjoint_field = lax.psum(deposit(incoming, total_cells), 'mem')]
    unnamed x3 -> x0, waiting for transfers between devices: 50.3 us -> none
    scatter-add x1 -> x0, other arithmetic: 41 us -> none  [deposit(): return jnp.zeros((total_cells,), jnp.float32).at[cells].add(lists[0])]
    slice x18 -> x8, local copies, waits for them, and re-layouts: 22 us -> 9.05 us  [the longest x4 4.04 us: on_device(): flux = coef[..., :-1] * (value[..., 1:] - value[..., :-1])]
    ppermute x12 -> x2, local copies, waits for them, and re-layouts: 13.1 us -> 2.78 us  [the longest x1 2.35 us: on_device(): right = lax.ppermute(product[..., :halo], 'tile', backward)]
    scatter x1 -> x0, local copies, waits for them, and re-layouts: 6.73 us -> none  [on_device(): jnp.zeros((2, tiles * capacity), jnp.float32).at[:, slot].set(packed)]
    select_n x2 -> x9, other arithmetic: 0.74 us -> 7.47 us  [the longest x4 6.64 us: deposit(): jnp.where(hit, high[:, None], zero)]
    dot_general x0 -> x4, matrix products: none -> 6.63 us  [deposit(): jnp.einsum('nr,nj->rj', row_hit, weighted, preferred_element_type=jnp.flo...]
  transfers between devices with their start and end apart: 14 -> 11, of which waited for: 12 -> 7; matrix products, arithmetic and copies ran while one was open for 3% -> 10% of each run, Pallas kernels for 0% -> 0%
where the time goes in v1:
time: 113 us; the launch traced here: 112 us
  other arithmetic  28.5 us (25%)
  waiting for transfers between devices  27.4 us (24%)
  starting transfers between devices  20.4 us (18%)
  local copies, waits for them, and re-layouts  15.3 us (14%)
  blocking collectives  13.2 us (12%)
  matrix products  6.63 us (6%)
    all_to_all x1, blocking collectives, on_device(): summed = lax.all_to_all(blocks, 'mem', 0, 0, tiled=True).sum(axis=0)  13.2 us
    ppermute x3, waiting for transfers between devices, allreduce_mem(): x = keep + lax.ppermute(send, 'mem', pairs)  8.3 us
    sub x6, other arithmetic, on_device(): value = value[..., 1:-1] + flux[..., 1:] - flux[..., :-1]  8.05 us
    ppermute x1, waiting for transfers between devices, on_device(): coef_left = lax.ppermute(coef_x[..., -halo:], 'tile', forward)  7.2 us
    select_n x4, other arithmetic, deposit(): jnp.where(hit, high[:, None], zero)  6.64 us
    dot_general x4, matrix products, deposit(): jnp.einsum('nr,nj->rj', row_hit, weighted, preferred_element_type=jnp.flo...  6.63 us
    all_to_all x1, starting transfers between devices, on_device(): incoming = lax.all_to_all(outgoing, 'tile', 0, 0, tiled=True)  6.35 us
    ppermute x3, waiting for transfers between devices, allreduce_mem(): other = lax.ppermute(x, 'mem', pairs)  6.17 us
  transfers between devices with their start and end apart: 11, of which 7 were waited for; matrix products, arithmetic and copies ran while one was open for 10% of the time, Pallas kernels for 0%

profile of v1, /device:TPU:0, one launch (start us, length us, event | category | flops | bytes accessed | tf_op | source)
XLA Modules:
  0.0 112.1 jit_solution(7379487019639546033)
XLA Ops:
  2.2 6.3 %all-to-all-start = ((f32[4,2,2048]{2,1,0:T(2,128)}), f32[4,2,2048]{2,1,0:T(2,128)S(1)}, u32[]{:S(2)}, u32[]{:S(2)}) async-start(f32[4,2,2048]{2,1,0:T(2,128)} %pad_maximum_fusion.3), calls=%async_computation | async-start | bytes 131072 | tf_op jit(solution)/shard_map/all_to_all | solution.py:80
  8.5 5.7 %all-to-all-done = f32[4,2,2048]{2,1,0:T(2,128)S(1)} async-done(((f32[4,2,2048]{2,1,0:T(2,128)}), f32[4,2,2048]{2,1,0:T(2,128)S(1)}, u32[]{:S(2)}, u32[]{:S(2)}) %all-to-all-start) | async-done | bytes 65568 | tf_op jit(solution)/shard_map/all_to_all | solution.py:80
  14.5 1.7 %fusion.23 = (bf16[2048,512]{1,0:T(8,128)(2,1)S(1)}, bf16[2048,512]{1,0:T(8,128)(2,1)S(1)}) fusion(s32[2048]{0:T(1024)S(1)} %get-tuple-element.20, bf16[2048]{0:T(1024)(128)(2,1)S(1)} %get-tuple-element.23, bf16[2048]{0:T(1024)(128)(2,1)S(1)} %get-tuple-element.24), kind=kLoop, calls=%fused_computation.27 | loop fusion | flops 3145728 | bytes 4210688 | tf_op jit(solution)/shard_map/jit(_where)/select_n | solution.py:34
  16.1 1.6 %fusion = f32[256,1024]{1,0:T(8,128)S(1)} fusion(bf16[2048,512]{1,0:T(8,128)(2,1)S(1)} %get-tuple-element.22, bf16[2048,512]{1,0:T(8,128)(2,1)S(1)} %get-tuple-element.21, s32[2048]{0:T(1024)S(1)} %get-tuple-element.19), kind=kOutput, calls=%fused_computation | convolution fusion | flops 1082654720 | bytes 5251072 | tf_op jit(solution)/shard_map/nr,nj->rj/dot_general | solution.py:36
  17.8 1.7 %fusion.21 = (bf16[2048,512]{1,0:T(8,128)(2,1)S(1)}, bf16[2048,512]{1,0:T(8,128)(2,1)S(1)}) fusion(s32[2048]{0:T(1024)S(1)} %get-tuple-element.26, bf16[2048]{0:T(1024)(128)(2,1)S(1)} %get-tuple-element.29, bf16[2048]{0:T(1024)(128)(2,1)S(1)} %get-tuple-element.30), kind=kLoop, calls=%fused_computation.24 | loop fusion | flops 3145728 | bytes 4210688 | tf_op jit(solution)/shard_map/jit(_where)/select_n | solution.py:34
  19.5 1.7 %fusion.4 = f32[256,1024]{1,0:T(8,128)S(1)} fusion(bf16[2048,512]{1,0:T(8,128)(2,1)S(1)} %get-tuple-element.28, bf16[2048,512]{1,0:T(8,128)(2,1)S(1)} %get-tuple-element.27, s32[2048]{0:T(1024)S(1)} %get-tuple-element.25), kind=kOutput, calls=%fused_computation.4 | convolution fusion | flops 1082654720 | bytes 5251072 | tf_op jit(solution)/shard_map/nr,nj->rj/dot_general | solution.py:36
  21.1 1.7 %fusion.19 = (bf16[2048,512]{1,0:T(8,128)(2,1)S(1)}, bf16[2048,512]{1,0:T(8,128)(2,1)S(1)}) fusion(s32[2048]{0:T(1024)S(1)} %get-tuple-element.32, bf16[2048]{0:T(1024)(128)(2,1)S(1)} %get-tuple-element.35, bf16[2048]{0:T(1024)(128)(2,1)S(1)} %get-tuple-element.36), kind=kLoop, calls=%fused_computation.21 | loop fusion | flops 3145728 | bytes 4210688 | tf_op jit(solution)/shard_map/jit(_where)/select_n | solution.py:34
  22.8 1.7 %fusion.8 = f32[256,1024]{1,0:T(8,128)S(1)} fusion(bf16[2048,512]{1,0:T(8,128)(2,1)S(1)} %get-tuple-element.34, bf16[2048,512]{1,0:T(8,128)(2,1)S(1)} %get-tuple-element.33, s32[2048]{0:T(1024)S(1)} %get-tuple-element.31), kind=kOutput, calls=%fused_computation.8 | convolution fusion | flops 1082654720 | bytes 5251072 | tf_op jit(solution)/shard_map/nr,nj->rj/dot_general | solution.py:36
  24.5 1.7 %fusion.17 = (bf16[2048,512]{1,0:T(8,128)(2,1)S(1)}, bf16[2048,512]{1,0:T(8,128)(2,1)S(1)}) fusion(s32[2048]{0:T(1024)S(1)} %get-tuple-element.38, bf16[2048]{0:T(1024)(128)(2,1)S(1)} %get-tuple-element.41, bf16[2048]{0:T(1024)(128)(2,1)S(1)} %get-tuple-element.42), kind=kLoop, calls=%fused_computation.18 | loop fusion | flops 3145728 | bytes 4210688 | tf_op jit(solution)/shard_map/jit(_where)/select_n | solution.py:34
  26.1 1.7 %fusion.12 = f32[256,1024]{1,0:T(8,128)S(1)} fusion(bf16[2048,512]{1,0:T(8,128)(2,1)S(1)} %get-tuple-element.40, bf16[2048,512]{1,0:T(8,128)(2,1)S(1)} %get-tuple-element.39, s32[2048]{0:T(1024)S(1)} %get-tuple-element.37), kind=kOutput, calls=%fused_computation.12 | convolution fusion | flops 1082654720 | bytes 5251072 | tf_op jit(solution)/shard_map/nr,nj->rj/dot_general | solution.py:36
  28.4 1.5 %collective-permute-done = f32[128,512]{1,0:T(8,128)S(1)} collective-permute-done((f32[128,512]{1,0:T(8,128)S(1)}, f32[128,512]{1,0:T(8,128)S(1)}, u32[]{:S(2)}, u32[]{:S(2)}) %collective-permute-start) | collective-permute-done | bytes 262176 | tf_op jit(solution)/shard_map/ppermute | solution.py:50
  30.0 1.6 %collective-permute-start.1 = (f32[64,512]{1,0:T(8,128)S(1)}, f32[64,512]{1,0:T(8,128)S(1)}, u32[]{:S(2)}, u32[]{:S(2)}) collective-permute-start(f32[64,512]{1,0:T(8,128)S(1)} %dynamic-slice_bitcast_fusion.1), channel_id=1, source_target_pairs={{0,8},{4,12},{8,0},{12,4},{16,24},{20,28},{24,16},{28,20},{1,9},{5... | collective-permute-start | bytes 393224 | tf_op jit(solution)/shard_map/ppermute | solution.py:50
  31.6 4.0 %collective-permute-done.1 = f32[64,512]{1,0:T(8,128)S(1)} collective-permute-done((f32[64,512]{1,0:T(8,128)S(1)}, f32[64,512]{1,0:T(8,128)S(1)}, u32[]{:S(2)}, u32[]{:S(2)}) %collective-permute-start.1) | collective-permute-done | bytes 131104 | tf_op jit(solution)/shard_map/ppermute | solution.py:50
  35.7 1.6 %collective-permute-start.2 = (f32[32,512]{1,0:T(8,128)S(1)}, f32[32,512]{1,0:T(8,128)S(1)}, u32[]{:S(2)}, u32[]{:S(2)}) collective-permute-start(f32[32,512]{1,0:T(8,128)S(1)} %dynamic-slice_bitcast_fusion.2), channel_id=1, source_target_pairs={{0,16},{4,20},{8,24},{12,28},{16,0},{20,4},{24,8},{28,12},{1,17},{... | collective-permute-start | bytes 196616 | tf_op jit(solution)/shard_map/ppermute | solution.py:50
  37.2 2.7 %collective-permute-done.2 = f32[32,512]{1,0:T(8,128)S(1)} collective-permute-done((f32[32,512]{1,0:T(8,128)S(1)}, f32[32,512]{1,0:T(8,128)S(1)}, u32[]{:S(2)}, u32[]{:S(2)}) %collective-permute-start.2) | collective-permute-done | bytes 65568 | tf_op jit(solution)/shard_map/ppermute | solution.py:50
  40.0 1.6 %collective-permute-start.3 = (f32[32,512]{1,0:T(8,128)S(1)}, f32[32,512]{1,0:T(8,128)S(1)}, u32[]{:S(2)}, u32[]{:S(2)}) collective-permute-start(f32[32,512]{1,0:T(8,128)S(1)} %get-tuple-element.6), channel_id=1, source_target_pairs={{0,16},{4,20},{8,24},{12,28},{16,0},{20,4},{24,8},{28,12},{1,17},{... | collective-permute-start | bytes 196616 | tf_op jit(solution)/shard_map/ppermute | solution.py:54
  41.6 2.7 %collective-permute-done.3 = f32[32,512]{1,0:T(8,128)S(1)} collective-permute-done((f32[32,512]{1,0:T(8,128)S(1)}, f32[32,512]{1,0:T(8,128)S(1)}, u32[]{:S(2)}, u32[]{:S(2)}) %collective-permute-start.3) | collective-permute-done | bytes 65568 | tf_op jit(solution)/shard_map/ppermute | solution.py:54
  44.4 1.6 %collective-permute-start.4 = (f32[64,512]{1,0:T(8,128)S(1)}, f32[64,512]{1,0:T(8,128)S(1)}, u32[]{:S(2)}, u32[]{:S(2)}) collective-permute-start(f32[64,512]{1,0:T(8,128)S(1)} %bitcast.68), channel_id=1, source_target_pairs={{0,8},{4,12},{8,0},{12,4},{16,24},{20,28},{24,16},{28,20},{1,9},{5... | collective-permute-start | bytes 393224 | tf_op jit(solution)/shard_map/ppermute | solution.py:54
  46.0 3.4 %collective-permute-done.4 = f32[64,512]{1,0:T(8,128)S(1)} collective-permute-done((f32[64,512]{1,0:T(8,128)S(1)}, f32[64,512]{1,0:T(8,128)S(1)}, u32[]{:S(2)}, u32[]{:S(2)}) %collective-permute-start.4) | collective-permute-done | bytes 131104 | tf_op jit(solution)/shard_map/ppermute | solution.py:54
  51.2 2.9 %collective-permute-start.9 = (f32[2,256,6]{2,1,0:T(8,128)}, f32[2,256,6]{2,1,0:T(8,128)S(1)}, u32[]{:S(2)}, u32[]{:S(2)}) collective-permute-start(f32[2,256,6]{2,1,0:T(8,128)} %get-tuple-element.10), channel_id=1, source_target_pairs={{1,0},{2,1},{3,2},{0,3},{5,4},{6,5},{7,6},{4,7},{9,8},{10,9},{11,1... | collective-permute-start | bytes 36872 | tf_op jit(solution)/shard_map/ppermute | solution.py:73
  54.1 7.2 %collective-permute-done.8 = f32[2,256,6]{2,1,0:T(8,128)S(1)} collective-permute-done((f32[2,256,6]{2,1,0:T(8,128)S(1)}, f32[2,256,6]{2,1,0:T(8,128)S(1)}, u32[]{:S(2)}, u32[]{:S(2)}) %collective-permute-start.8) | collective-permute-done | bytes 12320 | tf_op jit(solution)/shard_map/ppermute | solution.py:72
  64.0 1.5 %fusion.75 = (f32[5,2,256,6]{3,2,1,0:T(8,128)}, f32[5,2,256,6]{3,2,1,0:T(8,128)S(1)}) fusion(f32[5,2,256,128]{3,2,1,0:T(8,128)S(1)} %multiply_reduce_fusion.1), kind=kLoop, calls=%fused_computation.197 | loop fusion | bytes 245760 | tf_op jit(solution)/shard_map/slice | solution.py:89
  65.5 1.7 %copy.26 = f32[5,2,256,6]{2,1,3,0:T(2,128)S(1)} copy(f32[5,2,256,6]{3,2,1,0:T(8,128)} %get-tuple-element.7) | data formatting | bytes 122880 | tf_op jit(solution)/shard_map/slice | solution.py:89
  68.3 3.8 %collective-permute-start.7 = (f32[5,2,256,6]{2,1,3,0:T(2,128)}, f32[5,2,256,6]{2,1,3,0:T(2,128)}, u32[]{:S(2)}, u32[]{:S(2)}) collective-permute-start(f32[5,2,256,6]{2,1,3,0:T(2,128)} %copy.27), channel_id=1, source_target_pairs={{1,0},{2,1},{3,2},{0,3},{5,4},{6,5},{7,6},{4,7},{9,8},{10,9},{11,1... | collective-permute-start | bytes 184328 | tf_op jit(solution)/shard_map/ppermute | solution.py:90
  76.9 2.3 %copy.29 = f32[5,2,256,6]{3,2,1,0:T(8,128)} copy(f32[5,2,256,6]{2,1,3,0:T(2,128)} %collective-permute-done.7) | data formatting | bytes 122880 | tf_op jit(solution)/shard_map/ppermute | solution.py:90
  79.2 2.4 %pad_maximum_fusion = f32[5,2,256,140]{3,2,1,0:T(8,128)S(1)} fusion(f32[5,2,256,6]{3,2,1,0:T(8,128)} %copy.29, f32[5,2,256,128]{3,2,1,0:T(8,128)S(1)} %multiply_reduce_fusion.1, f32[5,2,256,6]{3,2,1,0:T(8,128)S(1)} %copy.28), kind=kLoop, calls=%fused_computation.50 | loop fusion | flops 716800 | bytes 2867200 | tf_op jit(solution)/shard_map/concatenate | solution.py:91
  82.4 1.4 %slice_subtract_fusion.9 = f32[5,2,256,138]{3,2,1,0:T(8,128)S(1)} fusion(f32[5,2,256,139]{3,2,1,0:T(8,128)S(1)} %fusion.29, f32[5,2,256,140]{3,2,1,0:T(8,128)S(1)} %pad_maximum_fusion), kind=kLoop, calls=%fused_computation.46 | loop fusion | flops 706560 | bytes 5652480 | tf_op jit(solution)/shard_map/sub | solution.py:95
  84.6 1.4 %slice_subtract_fusion.7 = f32[5,2,256,136]{3,2,1,0:T(8,128)S(1)} fusion(f32[5,2,256,137]{3,2,1,0:T(8,128)S(1)} %fusion.28, f32[5,2,256,138]{3,2,1,0:T(8,128)S(1)} %slice_subtract_fusion.9), kind=kLoop, calls=%fused_computation.42 | loop fusion | flops 696320 | bytes 5570560 | tf_op jit(solution)/shard_map/sub | solution.py:95
  86.8 1.4 %slice_subtract_fusion.5 = f32[5,2,256,134]{3,2,1,0:T(8,128)S(1)} fusion(f32[5,2,256,135]{3,2,1,0:T(8,128)S(1)} %fusion.27, f32[5,2,256,136]{3,2,1,0:T(8,128)S(1)} %slice_subtract_fusion.7), kind=kLoop, calls=%fused_computation.38 | loop fusion | flops 686080 | bytes 5488640 | tf_op jit(solution)/shard_map/sub | solution.py:95
  88.9 1.4 %slice_subtract_fusion.3 = f32[5,2,256,132]{3,2,1,0:T(8,128)S(1)} fusion(f32[5,2,256,133]{3,2,1,0:T(8,128)S(1)} %fusion.26, f32[5,2,256,134]{3,2,1,0:T(8,128)S(1)} %slice_subtract_fusion.5), kind=kLoop, calls=%fused_computation.34 | loop fusion | flops 675840 | bytes 5406720 | tf_op jit(solution)/shard_map/sub | solution.py:95
  91.1 1.6 %slice_subtract_fusion.1 = f32[5,2,256,130]{3,2,1,0:T(8,128)S(1)} fusion(f32[5,2,256,131]{3,2,1,0:T(8,128)S(1)} %fusion.25, f32[5,2,256,132]{3,2,1,0:T(8,128)S(1)} %slice_subtract_fusion.3), kind=kLoop, calls=%fused_computation.30 | loop fusion | flops 665600 | bytes 5324800 | tf_op jit(solution)/shard_map/sub | solution.py:95
  98.2 13.2 %all_to_all.10 = f32[8,32,2,2,128]{4,1,3,2,0:T(8,128)S(1)} all-to-all(f32[8,32,2,2,128]{4,1,3,2,0:T(8,128)S(1)} %copy.30), channel_id=1, replica_groups=mesh['mem'=8,'tile'=4] {'mem'}, dimensions={0} | all-to-all | bytes 1048576 | tf_op jit(solution)/shard_map/all_to_all | solution.py:102
  (90 shorter events, 23.0 us)
Async XLA Ops:
  2.2 12.1 %all-to-all-start = ((f32[4,2,2048]{2,1,0:T(2,128)}), f32[4,2,2048]{2,1,0:T(2,128)S(1)}, u32[]{:S(2)}, u32[]{:S(2)}) async-start(f32[4,2,2048]{2,1,0:T(2,128)} %pad_maximum_fusion.3), calls=%async_computation | async-start | bytes 131072 | tf_op jit(solution)/shard_map/all_to_all | solution.py:80
  28.3 21.2 %copy-start.3 = (f32[2,256,128]{2,1,0:T(8,128)S(1)}, f32[2,256,128]{2,1,0:T(8,128)}, u32[]{:S(2)}) copy-start(f32[2,256,128]{2,1,0:T(8,128)} %param.7) | copy-start | bytes 786436
  28.3 1.6 %collective-permute-start = (f32[128,512]{1,0:T(8,128)S(1)}, f32[128,512]{1,0:T(8,128)S(1)}, u32[]{:S(2)}, u32[]{:S(2)}) collective-permute-start(f32[128,512]{1,0:T(8,128)S(1)} %dynamic-slice_bitcast_fusion), channel_id=1, source_target_pairs={{0,4},{4,0},{8,12},{12,8},{16,20},{20,16},{24,28},{28,24},{1,5},{5... | collective-permute-start | bytes 786440 | tf_op jit(solution)/shard_map/ppermute | solution.py:50
  30.0 5.6 %collective-permute-start.1 = (f32[64,512]{1,0:T(8,128)S(1)}, f32[64,512]{1,0:T(8,128)S(1)}, u32[]{:S(2)}, u32[]{:S(2)}) collective-permute-start(f32[64,512]{1,0:T(8,128)S(1)} %dynamic-slice_bitcast_fusion.1), channel_id=1, source_target_pairs={{0,8},{4,12},{8,0},{12,4},{16,24},{20,28},{24,16},{28,20},{1,9},{5... | collective-permute-start | bytes 393224 | tf_op jit(solution)/shard_map/ppermute | solution.py:50
  35.7 4.3 %collective-permute-start.2 = (f32[32,512]{1,0:T(8,128)S(1)}, f32[32,512]{1,0:T(8,128)S(1)}, u32[]{:S(2)}, u32[]{:S(2)}) collective-permute-start(f32[32,512]{1,0:T(8,128)S(1)} %dynamic-slice_bitcast_fusion.2), channel_id=1, source_target_pairs={{0,16},{4,20},{8,24},{12,28},{16,0},{20,4},{24,8},{28,12},{1,17},{... | collective-permute-start | bytes 196616 | tf_op jit(solution)/shard_map/ppermute | solution.py:50
  40.0 4.3 %collective-permute-start.3 = (f32[32,512]{1,0:T(8,128)S(1)}, f32[32,512]{1,0:T(8,128)S(1)}, u32[]{:S(2)}, u32[]{:S(2)}) collective-permute-start(f32[32,512]{1,0:T(8,128)S(1)} %get-tuple-element.6), channel_id=1, source_target_pairs={{0,16},{4,20},{8,24},{12,28},{16,0},{20,4},{24,8},{28,12},{1,17},{... | collective-permute-start | bytes 196616 | tf_op jit(solution)/shard_map/ppermute | solution.py:54
  44.4 5.0 %collective-permute-start.4 = (f32[64,512]{1,0:T(8,128)S(1)}, f32[64,512]{1,0:T(8,128)S(1)}, u32[]{:S(2)}, u32[]{:S(2)}) collective-permute-start(f32[64,512]{1,0:T(8,128)S(1)} %bitcast.68), channel_id=1, source_target_pairs={{0,8},{4,12},{8,0},{12,4},{16,24},{20,28},{24,16},{28,20},{1,9},{5... | collective-permute-start | bytes 393224 | tf_op jit(solution)/shard_map/ppermute | solution.py:54
  49.4 13.0 %collective-permute-start.5 = (f32[128,512]{1,0:T(8,128)S(1)}, f32[128,512]{1,0:T(8,128)S(1)}, u32[]{:S(2)}, u32[]{:S(2)}) collective-permute-start(f32[128,512]{1,0:T(8,128)S(1)} %bitcast.62), channel_id=1, source_target_pairs={{0,4},{4,0},{8,12},{12,8},{16,20},{20,16},{24,28},{28,24},{1,5},{5... | collective-permute-start | bytes 786440 | tf_op jit(solution)/shard_map/ppermute | solution.py:54
  50.3 11.0 %collective-permute-start.8 = (f32[2,256,6]{2,1,0:T(8,128)S(1)}, f32[2,256,6]{2,1,0:T(8,128)S(1)}, u32[]{:S(2)}, u32[]{:S(2)}) collective-permute-start(f32[2,256,6]{2,1,0:T(8,128)S(1)} %get-tuple-element.9), channel_id=1, source_target_pairs={{0,1},{1,2},{2,3},{3,0},{4,5},{5,6},{6,7},{7,4},{8,9},{9,10},{10,1... | collective-permute-start | bytes 36872 | tf_op jit(solution)/shard_map/ppermute | solution.py:72
  51.2 20.9 %collective-permute-start.9 = (f32[2,256,6]{2,1,0:T(8,128)}, f32[2,256,6]{2,1,0:T(8,128)S(1)}, u32[]{:S(2)}, u32[]{:S(2)}) collective-permute-start(f32[2,256,6]{2,1,0:T(8,128)} %get-tuple-element.10), channel_id=1, source_target_pairs={{1,0},{2,1},{3,2},{0,3},{5,4},{6,5},{7,6},{4,7},{9,8},{10,9},{11,1... | collective-permute-start | bytes 36872 | tf_op jit(solution)/shard_map/ppermute | solution.py:73
  62.4 1.3 %copy-start.1 = (bf16[5,2,2,256,128]{4,3,2,1,0:T(8,128)(2,1)S(1)}, bf16[5,2,2,256,128]{4,3,2,1,0:T(8,128)(2,1)}, u32[]{:S(2)}) copy-start(bf16[5,2,2,256,128]{4,3,2,1,0:T(8,128)(2,1)} %param.6) | copy-start | bytes 3932164
  67.2 9.2 %collective-permute-start.6 = (f32[5,2,256,6]{2,1,3,0:T(2,128)S(1)}, f32[5,2,256,6]{2,1,3,0:T(2,128)S(1)}, u32[]{:S(2)}, u32[]{:S(2)}) collective-permute-start(f32[5,2,256,6]{2,1,3,0:T(2,128)S(1)} %copy.26), channel_id=1, source_target_pairs={{0,1},{1,2},{2,3},{3,0},{4,5},{5,6},{6,7},{7,4},{8,9},{9,10},{10,1... | collective-permute-start | bytes 184328 | tf_op jit(solution)/shard_map/ppermute | solution.py:89
  68.3 8.6 %collective-permute-start.7 = (f32[5,2,256,6]{2,1,3,0:T(2,128)}, f32[5,2,256,6]{2,1,3,0:T(2,128)}, u32[]{:S(2)}, u32[]{:S(2)}) collective-permute-start(f32[5,2,256,6]{2,1,3,0:T(2,128)} %copy.27), channel_id=1, source_target_pairs={{1,0},{2,1},{3,2},{0,3},{5,4},{6,5},{7,6},{4,7},{9,8},{10,9},{11,1... | collective-permute-start | bytes 184328 | tf_op jit(solution)/shard_map/ppermute | solution.py:90
  82.4 1.4 %copy-start.8 = (f32[2,256,137]{2,1,0:T(8,128)S(1)}, f32[2,256,137]{2,1,0:T(8,128)}, u32[]{:S(2)}) copy-start(f32[2,256,137]{2,1,0:T(8,128)} %slice.321) | copy-start | bytes 841732
  84.6 1.4 %copy-start.7 = (f32[2,256,135]{2,1,0:T(8,128)S(1)}, f32[2,256,135]{2,1,0:T(8,128)}, u32[]{:S(2)}) copy-start(f32[2,256,135]{2,1,0:T(8,128)} %slice.327) | copy-start | bytes 829444
  86.7 1.4 %copy-start.6 = (f32[2,256,133]{2,1,0:T(8,128)S(1)}, f32[2,256,133]{2,1,0:T(8,128)}, u32[]{:S(2)}) copy-start(f32[2,256,133]{2,1,0:T(8,128)} %slice.333) | copy-start | bytes 817156
  88.9 1.4 %copy-start.5 = (f32[2,256,131]{2,1,0:T(8,128)S(1)}, f32[2,256,131]{2,1,0:T(8,128)}, u32[]{:S(2)}) copy-start(f32[2,256,131]{2,1,0:T(8,128)} %slice.339) | copy-start | bytes 804868
  91.1 1.6 %copy-start.4 = (f32[2,256,129]{2,1,0:T(8,128)S(1)}, f32[2,256,129]{2,1,0:T(8,128)}, u32[]{:S(2)}) copy-start(f32[2,256,129]{2,1,0:T(8,128)} %pad_maximum_fusion.1) | copy-start | bytes 792580
  93.5 1.0 copy-start
  96.5 1.3 %copy-start.2 = (bf16[5,2,2,256,128]{4,3,2,1,0:T(8,128)(2,1)S(1)}, bf16[5,2,2,256,128]{4,3,2,1,0:T(8,128)(2,1)}, u32[]{:S(2)}) copy-start(bf16[5,2,2,256,128]{4,3,2,1,0:T(8,128)(2,1)} %param.6) | copy-start | bytes 3932164
